TPU v7x, 32 devices: a whole 2x2x4 slice. The times are simulated.
32 devices in a mesh: slab: 2 (over y), genome: 4 (over x, core), group: 4 (over z).
Axes of the slice: x: 2, y: 2, z: 4, core: 2. Of those that a mesh axis runs over, the one named last changes fastest.
Arguments:
- genotypes: bfloat16 [640, 12288], P(None, ('slab', 'genome', 'group')), parts along dimension 1, may hold values from -6 to 6
Outputs:
- ld_score: float32 [12288], P(('slab', 'genome', 'group')), parts along dimension 0
There are 2 independent parts, one for each index of `slab`. A program takes and returns all parts, laid end to end along the dimension named above; each array names one. Nothing has to cross between parts.
All inputs are finite; a program needn't handle non-finite values.
Results may differ from a plain program's by a relative error of at most 0.0003.
Values may be sent and summed in bfloat16 or wider, within the bound.
No kernel may reach another device: no remote copies, remote signals or barrier semaphores. Data moves between devices by JAX's collectives and lax.ppermute only.
A program may use at most 64 MiB of HBM per device.

v0:
```python
import jax
import jax.numpy as jnp
from jax import lax
from jax.sharding import PartitionSpec as P


def passed_along(block, axis, distance):
    devices = range(lax.axis_size(axis))
    route = [(i - distance, i) for i in devices if i - distance in devices]
    return lax.ppermute(block, axis, route)


def per_device(genotypes):
    scaling = 1.0 / genotypes.shape[0]

    def squares(columns):
        band = (
            lax.dot_general(
                genotypes, columns, (((0,), (0,)), ((), ())), preferred_element_type=jnp.float32
            )
            * scaling
        )
        return jnp.sum(band * band, axis=1)

    gathered = lax.all_gather(genotypes, "group", axis=1, tiled=True)
    following = passed_along(gathered, "genome", -1)
    ld_score = squares(gathered) + squares(following)
    return ld_score


def solution(mesh):
    placed = (P(None, ("slab", "genome", "group")),)
    return jax.shard_map(
        per_device,
        mesh=mesh,
        in_specs=placed,
        out_specs=P(("slab", "genome", "group")),
        check_vma=False,
    )
```

profile of v0, /device:TPU:1, one launch (start us, length us, event | category | flops | bytes accessed | tf_op | source)
XLA Modules:
  0.0 89.7 jit_solution(2843091351955072725)
XLA Ops:
  6.5 0.0 all-gather.2.cloned.1.call-start
  6.5 0.0 copy-start
  6.5 0.7 all-gather.2.cloned.1.call-update
  7.3 47.5 %all-gather.2.cloned.1.call-done = bf16[640,1536]{1,0:T(8,128)(2,1)} async-done(((bf16[640,384]{1,0:T(8,128)(2,1)}), bf16[640,1536]{1,0:T(8,128)(2,1)}) %all-gather.2.cloned.1.call-update) | async-done | bytes 1966096 | tf_op jit(solution)/shard_map/all_gather | solution.py:25
  54.7 2.7 %collective-permute-start = (bf16[640,1536]{1,0:T(8,128)(2,1)}, bf16[640,1536]{1,0:T(8,128)(2,1)S(1)}, u32[]{:S(2)}, u32[]{:S(2)}) collective-permute-start(bf16[640,1536]{1,0:T(8,128)(2,1)} %all-gather.2.cloned.1.call-done), channel_id=1, source_target_pairs={{4,0},{8,4},{12,8},{5,1},{9,5},{13,9},{6,2},{10,6},{14,10},{7,3},{... | collective-permute-start | bytes 5898248 | tf_op jit(solution)/shard_map/ppermute | solution.py:10
  57.5 2.9 %fusion.2 = f32[384]{0:T(512)S(1)} fusion(bf16[640,384]{1,0:T(8,128)(2,1)} %param.1, bf16[640,1536]{1,0:T(8,128)(2,1)} %all-gather.2.cloned.1.call-done), kind=kOutput, calls=%fused_computation.4 | convolution fusion | flops 756743808 | bytes 2459136 | tf_op jit(solution)/shard_map/dot_general | solution.py:18
  60.4 20.7 %collective-permute-done = bf16[640,1536]{1,0:T(8,128)(2,1)S(1)} collective-permute-done((bf16[640,1536]{1,0:T(8,128)(2,1)}, bf16[640,1536]{1,0:T(8,128)(2,1)S(1)}, u32[]{:S(2)}, u32[]{:S(2)}) %collective-permute-start) | collective-permute-done | bytes 1966112 | tf_op jit(solution)/shard_map/ppermute | solution.py:10
  81.1 0.0 copy-done
  81.1 1.2 %fusion.3 = f32[384]{0:T(512)S(1)} fusion(bf16[640,384]{1,0:T(8,128)(2,1)S(1)} %copy-done, bf16[640,1536]{1,0:T(8,128)(2,1)S(1)} %collective-permute-done), kind=kOutput, calls=%fused_computation.5 | convolution fusion | flops 756743808 | bytes 2459136 | tf_op jit(solution)/shard_map/dot_general | solution.py:18
  82.2 0.6 add.3
Async XLA Ops:
  6.5 48.2 %all-gather.2.cloned.1.call-start = ((), (), s32[]{:S(2)}) async-start(), calls=%async_computation | async-start | bytes 2457600 | tf_op jit(solution)/shard_map/all_gather | solution.py:25
  6.5 74.5 %copy-start = (bf16[640,384]{1,0:T(8,128)(2,1)S(1)}, bf16[640,384]{1,0:T(8,128)(2,1)}, u32[]{:S(2)}) copy-start(bf16[640,384]{1,0:T(8,128)(2,1)} %param.1) | copy-start | bytes 1474564
  54.7 26.3 %collective-permute-start = (bf16[640,1536]{1,0:T(8,128)(2,1)}, bf16[640,1536]{1,0:T(8,128)(2,1)S(1)}, u32[]{:S(2)}, u32[]{:S(2)}) collective-permute-start(bf16[640,1536]{1,0:T(8,128)(2,1)} %all-gather.2.cloned.1.call-done), channel_id=1, source_target_pairs={{4,0},{8,4},{12,8},{5,1},{9,5},{13,9},{6,2},{10,6},{14,10},{7,3},{... | collective-permute-start | bytes 5898248 | tf_op jit(solution)/shard_map/ppermute | solution.py:10
Sparse Core Ops, SparseCore 0:
  9.0 45.7 all-gather.1
where the time goes:
time: 89.8 us; the launch traced here: 89.7 us
  waiting for transfers between devices  68.8 us (77%)
  between operations  13.4 us (15%)
  matrix products  4.09 us (5%)
  starting transfers between devices  2.75 us (3%)
    all_gather x1, waiting for transfers between devices, per_device(): gathered = lax.all_gather(genotypes, 'group', axis=1, tiled=True)  47.5 us
    ppermute x1, waiting for transfers between devices, passed_along(): return lax.ppermute(block, axis, route)  20.7 us
    dot_general x2, matrix products, squares(): lax.dot_general(genotypes, columns, (((0,), (0,)), ((), ())), preferred_e...  4.09 us
    ppermute x1, starting transfers between devices, passed_along(): return lax.ppermute(block, axis, route)  2.75 us
  transfers between devices with their start and end apart: 2, of which 2 were waited for; matrix products, arithmetic and copies ran while one was open for 3% of the time, Pallas kernels for 0%

commit v1 on v0

--- a/solution.py
+++ b/solution.py
@@ -22,7 +22,14 @@
         )
         return jnp.sum(band * band, axis=1)
 
-    gathered = lax.all_gather(genotypes, "group", axis=1, tiled=True)
+    ring = [genotypes]
+    for hop in range(3):
+        ring.append(lax.ppermute(ring[-1], "group", [(dev, (dev + 1) % 4) for dev in range(4)]))
+    gathered = jnp.roll(
+        jnp.concatenate(ring[::-1], axis=1),
+        (lax.axis_index("group") + 1) * ring[0].shape[1],
+        axis=1,
+    )
     following = passed_along(gathered, "genome", -1)
     ld_score = squares(gathered) + squares(following)
     return ld_score

time: 89.8 us -> 74.3 us (0.83)
  between operations: 13.4 us -> 0.1 us
  waiting for transfers between devices: 68.8 us -> 60.6 us
  starting transfers between devices: 2.75 us -> 7.11 us
  local copies, waits for them, and re-layouts: 0.01 us -> 3.07 us
  matrix products: 4.09 us -> 2.69 us
    all_gather x1 -> x0, waiting for transfers between devices: 47.5 us -> none  [per_device(): gathered = lax.all_gather(genotypes, 'group', axis=1, tiled=True)]
    ppermute x0 -> x3, waiting for transfers between devices: none -> 38.9 us  [per_device(): lax.ppermute(ring[-1], 'group', [(dev, (dev + 1) % 4) for dev in range(4)])]
    ppermute x1, starting transfers between devices: 2.75 us -> 4.98 us  [passed_along(): return lax.ppermute(block, axis, route)]
    ppermute x0 -> x3, starting transfers between devices: none -> 2.13 us  [per_device(): lax.ppermute(ring[-1], 'group', [(dev, (dev + 1) % 4) for dev in range(4)])]
    unnamed x2 -> x9, local copies, waits for them, and re-layouts: 0.01 us -> 1.8 us
    dot_general x2, matrix products: 4.09 us -> 2.69 us  [squares(): lax.dot_general(genotypes, columns, (((0,), (0,)), ((), ())), preferred_e...]
    dynamic_slice x0 -> x1, local copies, waits for them, and re-layouts: none -> 1.15 us  [per_device(): jnp.roll(jnp.concatenate(ring[::-1], axis=1), (lax.axis_index('group') +...]
    ppermute x1, waiting for transfers between devices: 20.7 us -> 21.7 us  [passed_along(): return lax.ppermute(block, axis, route)]
  transfers between devices with their start and end apart: 2 -> 4, of which waited for: 2 -> 4; matrix products, arithmetic and copies ran while one was open for 3% -> 2% of each run, Pallas kernels for 0% -> 0%
where the time goes in v1:
time: 74.3 us; the launch traced here: 74.1 us
  waiting for transfers between devices  60.6 us (82%)
  starting transfers between devices  7.11 us (10%)
  local copies, waits for them, and re-layouts  3.07 us (4%)
  matrix products  2.69 us (4%)
    ppermute x3, waiting for transfers between devices, per_device(): lax.ppermute(ring[-1], 'group', [(dev, (dev + 1) % 4) for dev in range(4)])  38.9 us
    ppermute x1, waiting for transfers between devices, passed_along(): return lax.ppermute(block, axis, route)  21.7 us
    ppermute x1, starting transfers between devices, passed_along(): return lax.ppermute(block, axis, route)  4.98 us
    dot_general x2, matrix products, squares(): lax.dot_general(genotypes, columns, (((0,), (0,)), ((), ())), preferred_e...  2.69 us
    ppermute x3, starting transfers between devices, per_device(): lax.ppermute(ring[-1], 'group', [(dev, (dev + 1) % 4) for dev in range(4)])  2.13 us
    unnamed x9, local copies, waits for them, and re-layouts  1.8 us
  transfers between devices with their start and end apart: 4, of which 4 were waited for; matrix products, arithmetic and copies ran while one was open for 2% of the time, Pallas kernels for 0%

profile of v1, /device:TPU:1, one launch (start us, length us, event | category | flops | bytes accessed | tf_op | source)
XLA Modules:
  0.0 74.1 jit_solution(3866035682635391593)
XLA Ops:
  0.0 0.0 copy-start
  0.0 2.1 %collective-permute-start = (bf16[640,384]{1,0:T(8,128)(2,1)}, bf16[640,384]{1,0:T(8,128)(2,1)S(1)}, u32[]{:S(2)}, u32[]{:S(2)}) collective-permute-start(bf16[640,384]{1,0:T(8,128)(2,1)} %param.1), channel_id=1, source_target_pairs={{0,1},{1,2},{2,3},{3,0},{4,5},{5,6},{6,7},{7,4},{8,9},{9,10},{10,1... | collective-permute-start | bytes 1474568 | tf_op jit(solution)/shard_map/ppermute | solution.py:27
  2.1 13.3 %collective-permute-done = bf16[640,384]{1,0:T(8,128)(2,1)S(1)} collective-permute-done((bf16[640,384]{1,0:T(8,128)(2,1)}, bf16[640,384]{1,0:T(8,128)(2,1)S(1)}, u32[]{:S(2)}, u32[]{:S(2)}) %collective-permute-start) | collective-permute-done | bytes 491552 | tf_op jit(solution)/shard_map/ppermute | solution.py:27
  15.4 0.0 collective-permute-start.1
  15.4 13.3 %collective-permute-done.1 = bf16[640,384]{1,0:T(8,128)(2,1)S(1)} collective-permute-done((bf16[640,384]{1,0:T(8,128)(2,1)S(1)}, bf16[640,384]{1,0:T(8,128)(2,1)S(1)}, u32[]{:S(2)}, u32[]{:S(2)}) %collective-permute-start.1) | collective-permute-done | bytes 491552 | tf_op jit(solution)/shard_map/ppermute | solution.py:27
  28.7 0.0 collective-permute-start.2
  28.7 12.4 %collective-permute-done.2 = bf16[640,384]{1,0:T(8,128)(2,1)S(1)} collective-permute-done((bf16[640,384]{1,0:T(8,128)(2,1)S(1)}, bf16[640,384]{1,0:T(8,128)(2,1)S(1)}, u32[]{:S(2)}, u32[]{:S(2)}) %collective-permute-start.2) | collective-permute-done | bytes 491552 | tf_op jit(solution)/shard_map/ppermute | solution.py:27
  41.0 0.1 constant_dynamic-update-slice_fusion.7
  41.1 0.1 constant_dynamic-update-slice_fusion.6
  41.2 0.1 constant_dynamic-update-slice_fusion.5
  41.4 1.1 %constant_dynamic-update-slice_fusion.4 = bf16[640,3072]{1,0:T(8,128)(2,1)S(1)} fusion(bf16[640,3072]{1,0:T(8,128)(2,1)S(1)} %constant_dynamic-update-slice_fusion.5, bf16[640,384]{1,0:T(8,128)(2,1)} %param.1), kind=kLoop, calls=%fused_computation.10 | loop fusion | bytes 983040
  42.5 0.1 constant_dynamic-update-slice_fusion.3
  42.6 0.1 constant_dynamic-update-slice_fusion.2
  42.8 0.1 constant_dynamic-update-slice_fusion.1
  42.9 0.0 copy-done
  42.9 0.1 constant_dynamic-update-slice_fusion
  43.0 1.2 %constant_dynamic-slice_fusion = bf16[640,1536]{1,0:T(8,128)(2,1)S(1)} fusion(bf16[640,3072]{1,0:T(8,128)(2,1)S(1)} %constant_dynamic-update-slice_fusion, s32[]{:T(128)S(6)} %select_n.14), kind=kLoop, calls=%fused_computation.14 | loop fusion | bytes 3932164 | tf_op jit(solution)/shard_map/jit(_roll_dynamic)/dynamic_slice | solution.py:28
  44.2 5.0 %collective-permute-start.3 = (bf16[640,1536]{1,0:T(8,128)(2,1)S(1)}, bf16[640,1536]{1,0:T(8,128)(2,1)S(1)}, u32[]{:S(2)}, u32[]{:S(2)}) collective-permute-start(bf16[640,1536]{1,0:T(8,128)(2,1)S(1)} %constant_dynamic-slice_fusion), channel_id=1, source_target_pairs={{4,0},{8,4},{12,8},{5,1},{9,5},{13,9},{6,2},{10,6},{14,10},{7,3},{... | collective-permute-start | bytes 5898248 | tf_op jit(solution)/shard_map/ppermute | solution.py:10
  49.2 1.3 %fusion.2 = f32[384]{0:T(512)S(1)} fusion(bf16[640,1536]{1,0:T(8,128)(2,1)S(1)} %constant_dynamic-slice_fusion, bf16[640,384]{1,0:T(8,128)(2,1)S(1)} %copy-done), kind=kOutput, calls=%fused_computation.4 | convolution fusion | flops 756743808 | bytes 2459136 | tf_op jit(solution)/shard_map/dot_general | solution.py:18
  50.5 21.7 %collective-permute-done.3 = bf16[640,1536]{1,0:T(8,128)(2,1)S(1)} collective-permute-done((bf16[640,1536]{1,0:T(8,128)(2,1)S(1)}, bf16[640,1536]{1,0:T(8,128)(2,1)S(1)}, u32[]{:S(2)}, u32[]{:S(2)}) %collective-permute-start.3) | collective-permute-done | bytes 1966112 | tf_op jit(solution)/shard_map/ppermute | solution.py:10
  72.2 1.3 %fusion.3 = f32[384]{0:T(512)S(1)} fusion(bf16[640,1536]{1,0:T(8,128)(2,1)S(1)} %collective-permute-done.3, bf16[640,384]{1,0:T(8,128)(2,1)S(1)} %copy-done), kind=kOutput, calls=%fused_computation.5 | convolution fusion | flops 756743808 | bytes 2459136 | tf_op jit(solution)/shard_map/dot_general | solution.py:18
  73.6 0.6 add.19
Async XLA Ops:
  0.0 42.9 %copy-start = (bf16[640,384]{1,0:T(8,128)(2,1)S(1)}, bf16[640,384]{1,0:T(8,128)(2,1)}, u32[]{:S(2)}) copy-start(bf16[640,384]{1,0:T(8,128)(2,1)} %param.1) | copy-start | bytes 1474564
  0.0 15.4 %collective-permute-start = (bf16[640,384]{1,0:T(8,128)(2,1)}, bf16[640,384]{1,0:T(8,128)(2,1)S(1)}, u32[]{:S(2)}, u32[]{:S(2)}) collective-permute-start(bf16[640,384]{1,0:T(8,128)(2,1)} %param.1), channel_id=1, source_target_pairs={{0,1},{1,2},{2,3},{3,0},{4,5},{5,6},{6,7},{7,4},{8,9},{9,10},{10,1... | collective-permute-start | bytes 1474568 | tf_op jit(solution)/shard_map/ppermute | solution.py:27
  15.4 13.3 %collective-permute-start.1 = (bf16[640,384]{1,0:T(8,128)(2,1)S(1)}, bf16[640,384]{1,0:T(8,128)(2,1)S(1)}, u32[]{:S(2)}, u32[]{:S(2)}) collective-permute-start(bf16[640,384]{1,0:T(8,128)(2,1)S(1)} %collective-permute-done), channel_id=1, source_target_pairs={{0,1},{1,2},{2,3},{3,0},{4,5},{5,6},{6,7},{7,4},{8,9},{9,10},{10,1... | collective-permute-start | bytes 1474568 | tf_op jit(solution)/shard_map/ppermute | solution.py:27
  28.7 12.4 %collective-permute-start.2 = (bf16[640,384]{1,0:T(8,128)(2,1)S(1)}, bf16[640,384]{1,0:T(8,128)(2,1)S(1)}, u32[]{:S(2)}, u32[]{:S(2)}) collective-permute-start(bf16[640,384]{1,0:T(8,128)(2,1)S(1)} %collective-permute-done.1), channel_id=1, source_target_pairs={{0,1},{1,2},{2,3},{3,0},{4,5},{5,6},{6,7},{7,4},{8,9},{9,10},{10,1... | collective-permute-start | bytes 1474568 | tf_op jit(solution)/shard_map/ppermute | solution.py:27
  44.2 28.0 %collective-permute-start.3 = (bf16[640,1536]{1,0:T(8,128)(2,1)S(1)}, bf16[640,1536]{1,0:T(8,128)(2,1)S(1)}, u32[]{:S(2)}, u32[]{:S(2)}) collective-permute-start(bf16[640,1536]{1,0:T(8,128)(2,1)S(1)} %constant_dynamic-slice_fusion), channel_id=1, source_target_pairs={{4,0},{8,4},{12,8},{5,1},{9,5},{13,9},{6,2},{10,6},{14,10},{7,3},{... | collective-permute-start | bytes 5898248 | tf_op jit(solution)/shard_map/ppermute | solution.py:10
